TPU v7x, 32 devices: a whole 2x2x4 slice. The times are simulated.
32 devices in a mesh: space: 8 (over y, x, core), species: 4 (over z).
Axes of the slice: x: 2, y: 2, z: 4, core: 2. Of those that a mesh axis runs over, the one named last changes fastest.
Arguments:
- cotangent: bfloat16 [4, 400, 20, 1024], P('species', None, None, 'space'), may hold values from -6 to 6
- freq: float32 [4], P('species'), may hold values from 0.2 to 0.9
- ratio: float32 [4], P('species'), may hold values from 0.5 to 1
- coupling: float32 [4, 4, 13], replicated, may hold values from 0.1 to 0.6
- wall: int32 [1024], P('space'), may hold values 0 or 1
- inlet: int32 [1024], P('space'), may hold values 0 or 1
- face_type: int32 [2, 8], P(None, 'space'), may hold values from 0 to 1
Outputs:
- grad_state: bfloat16 [4, 400, 20, 1024], P('species', None, None, 'space')
Inputs may be any that keep to these rules, and one draw needn't show every extreme that they name: `wall`: 1 marks a solid cell. `inlet`: 1 marks an inlet cell. `face_type`: 0 is a specular wall, 1 a reversing wall.
All inputs are finite; a program needn't handle non-finite values. No bound on the sum of `wall` or of `inlet` on one device may be relied on, other than what follows from the above.
Results may differ from a plain program's by a relative error of at most 0.0049.
Values may be sent and summed in bfloat16 or wider, within the bound.
No kernel may reach another device: no remote copies, remote signals or barrier semaphores. Data moves between devices by JAX's collectives and lax.ppermute only.
A program may use at most 64 MiB of HBM per device.

v0:
```python
import math

import numpy as np
import jax
import jax.numpy as jnp
from jax import lax
from jax.experimental import pallas as pl
from jax.experimental.pallas import tpu as pltpu
from jax.sharding import PartitionSpec as P


NZ = 128

courant_max = 0.45
node_reach = 2.85


def passed_along(value, axis, steps):
    count = lax.axis_size(axis)
    pairs = [(source, (source + steps) % count) for source in range(count)]
    return lax.ppermute(value, axis, pairs)


def velocity_tables(node_count):
    pair_count = node_count * node_count
    spacing = 2.0 * node_reach / (node_count - 1)
    node_line = (np.arange(node_count, dtype=np.float64) - 0.5 * (node_count - 1)) * spacing
    grid_shape = (pair_count, node_count)
    along_x = np.broadcast_to(np.repeat(node_line, node_count)[:, None], grid_shape)
    along_y = np.broadcast_to(np.tile(node_line, node_count)[:, None], grid_shape)
    along_z = np.broadcast_to(node_line[None, :], grid_shape)
    square = along_x * along_x + along_y * along_y + along_z * along_z
    heat_term = square - 2.5
    functions = [
        np.ones(grid_shape),
        along_x,
        along_y,
        along_z,
        square - 1.5,
        along_x * along_y,
        along_x * along_z,
        along_y * along_z,
        along_x * along_x - along_y * along_y,
        along_y * along_y - along_z * along_z,
        along_x * heat_term,
        along_y * heat_term,
        along_z * heat_term,
    ]
    stacked = np.stack(functions)
    basis = stacked / np.sqrt(np.mean(stacked * stacked, axis=(1, 2), keepdims=True))
    weights = np.exp(-square) * (spacing * spacing * spacing) / math.pi**1.5
    recon = basis * weights[None]
    return node_line, basis, recon


def bf16_split(table, parts):
    rest = np.asarray(table, np.float64)
    pieces = []
    for _ in range(parts):
        piece = rest.astype(np.float32).astype(jnp.bfloat16).astype(np.float64)
        pieces.append(piece)
        rest = rest - piece
    return pieces


def on_device(cotangent, freq, ratio, coupling, wall, inlet, face_type):
    pair_count = cotangent.shape[1]
    node_count = cotangent.shape[2]
    cell_count = cotangent.shape[3]
    assert cell_count == NZ
    half = pair_count // 2
    moment_count = coupling.shape[2]
    species_count = lax.axis_size("species")

    node_line, basis, recon = velocity_tables(node_count)
    basis_k = np.transpose(basis, (0, 2, 1)).reshape(moment_count, node_count * pair_count)
    basis_parts = np.concatenate(bf16_split(basis_k, 3), axis=0)
    basis_parts = jnp.asarray(basis_parts.astype(jnp.bfloat16))
    weight_k = (recon[0] / basis[0]).T.reshape(-1).astype(np.float32)

    field_in = jnp.transpose(cotangent[0], (1, 0, 2))
    upper_in = field_in[:, half:, :]
    lower_in = field_in[:, :half, :]
    got_next = passed_along(upper_in, "space", -1)
    got_prev = passed_along(lower_in, "space", 1)

    open_cells = (1 - wall).astype(jnp.float32)
    keep_upper = open_cells * (1.0 - inlet.astype(jnp.float32))
    upward = (jnp.arange(pair_count) >= half)[None, :, None]
    keep = jnp.where(upward, keep_upper[None, None, :], open_cells[None, None, :])
    masked = field_in * keep.astype(jnp.bfloat16)
    parts = jnp.dot(
        basis_parts,
        masked.reshape(node_count * pair_count, cell_count),
        preferred_element_type=jnp.float32,
    )
    moments = parts[:moment_count] + parts[moment_count : 2 * moment_count] + parts[2 * moment_count :]

    species_index = lax.axis_index("species")
    row_k = lax.dynamic_index_in_dim(coupling, species_index, axis=0, keepdims=False)
    own_weight = lax.dynamic_index_in_dim(row_k, species_index, axis=0, keepdims=False)
    cross = own_weight[:, None] * moments
    for shift in range(1, species_count):
        source = (species_index - shift) % species_count
        other = passed_along(moments, "species", shift)
        weight = lax.dynamic_index_in_dim(row_k, source, axis=0, keepdims=False)
        cross = cross + weight[:, None] * other

    rows = 16
    assert moment_count + 2 < rows
    packet = jnp.concatenate(
        [
            cross,
            open_cells[None],
            keep_upper[None],
            jnp.zeros((rows - moment_count - 2, cell_count), jnp.float32),
        ],
        axis=0,
    )
    packet_next = passed_along(packet, "space", -1)
    packet_prev = passed_along(packet, "space", 1)

    rate_value = freq[0]
    scale_factor = courant_max * ratio[0] / node_reach
    line = jnp.asarray(node_line.astype(np.float32))
    pair_line = jnp.repeat(line, node_count)
    adv_x = jnp.abs(scale_factor * pair_line)
    adv_z = jnp.abs(scale_factor * line)
    columns = jnp.broadcast_to(
        jnp.stack([1.0 - adv_x, adv_x])[:, :, None], (2, pair_count, cell_count)
    )
    scalars = jnp.concatenate(
        [adv_z, jnp.zeros((31 - node_count,), jnp.float32), (1.0 - rate_value)[None]]
    )
    faces = face_type[:, 0]

    basis_run = lax.optimization_barrier(basis_parts).astype(jnp.float32)
    basis_sum = (
        basis_run[:moment_count] + basis_run[moment_count : 2 * moment_count]
    ) + basis_run[2 * moment_count :]
    recon_all = basis_sum * jnp.asarray(weight_k)[None]
    r1 = recon_all.astype(jnp.bfloat16)
    rest = recon_all - r1.astype(jnp.float32)
    r2 = rest.astype(jnp.bfloat16)
    r3 = (rest - r2.astype(jnp.float32)).astype(jnp.bfloat16)
    lanes = 128
    order = [0, 0, 1, 0, 1, 2]
    place = np.zeros((3 * moment_count, lanes), np.float32)
    for block, part in enumerate(order):
        for m in range(moment_count):
            place[part * moment_count + m, block * rows + m] = 1.0
    stacked_parts = jnp.concatenate([r1, r2, r3], axis=0)
    recon_parts = lax.dot_general(
        stacked_parts,
        jnp.asarray(place, jnp.bfloat16),
        (((0,), (0,)), ((), ())),
        preferred_element_type=jnp.float32,
    ).astype(jnp.bfloat16).reshape(node_count, pair_count, lanes)

    flip_rows = lax.broadcasted_iota(jnp.int32, (pair_count, pair_count), 0)
    flip_cols = lax.broadcasted_iota(jnp.int32, (pair_count, pair_count), 1)
    flip = (flip_rows + flip_cols == pair_count - 1).astype(jnp.bfloat16)

    partial = own_kernel(field_in, recon_parts, packet, columns, flip, scalars, faces)
    out = halo_kernel(partial, got_next, got_prev, recon_parts, packet_next, packet_prev, columns, scalars)
    return jnp.transpose(out, (1, 0, 2))[None]


def cross_matrix(packet, moment_count):
    rows = packet.shape[0]
    row = lax.broadcasted_iota(jnp.int32, packet.shape, 0)
    values = jnp.where(row < moment_count, packet, 0.0)
    c1 = values.astype(jnp.bfloat16)
    left = values - c1.astype(jnp.float32)
    c2 = left.astype(jnp.bfloat16)
    c3 = (left - c2.astype(jnp.float32)).astype(jnp.bfloat16)
    pad = jnp.zeros((128 - 6 * rows, packet.shape[1]), jnp.bfloat16)
    return jnp.concatenate([c1, c2, c1, c3, c2, c1, pad], axis=0)


def own_kernel(field_in, recon_parts, packet, columns, flip, scalars, faces):
    node_count, pair_count, cell_count = field_in.shape
    half = pair_count // 2
    steps = node_count // 2
    moment_count = packet.shape[0] - 3

    def kernel(sc_ref, face_ref, cot_a, cot_b, rec_a, rec_b, pk_ref, col_ref, flip_ref, out_ref):
        j = pl.program_id(0)
        row = lax.broadcasted_iota(jnp.int32, (pair_count, cell_count), 0)
        lane = lax.broadcasted_iota(jnp.int32, (pair_count, cell_count), 1)
        pk = pk_ref[...]
        rate = sc_ref[31]
        keep = rate * jnp.where(row >= half, pk[moment_count + 1 : moment_count + 2, :], pk[moment_count : moment_count + 1, :])
        own = cross_matrix(pk, moment_count)

        def relax(values, rec):
            rebuilt = jnp.dot(rec, own, preferred_element_type=jnp.float32)
            return (keep * values.astype(jnp.float32) + rebuilt).astype(jnp.bfloat16)

        relaxed_a = relax(cot_a[0], rec_a[0])
        relaxed_b = relax(cot_b[0], rec_b[0])
        edges = jnp.where(lane == 0, relaxed_b, relaxed_a)
        flipped = jnp.dot(flip_ref[...], edges, preferred_element_type=jnp.float32)
        edges32 = edges.astype(jnp.float32)
        source_a = jnp.where(face_ref[0] == 1, flipped, edges32)
        source_b = jnp.where(face_ref[1] == 1, flipped, edges32)
        ra = relaxed_a.astype(jnp.float32)
        rb = relaxed_b.astype(jnp.float32)
        near_a = jnp.where(lane == 0, source_a, pltpu.roll(ra, 1, 1))
        near_b = jnp.where(lane == cell_count - 1, source_b, pltpu.roll(rb, cell_count - 1, 1))
        base = col_ref[0]
        zw_a = sc_ref[j]
        zw_b = sc_ref[node_count - 1 - j]
        out_ref[0, 0] = (base - zw_a) * ra + zw_a * near_a
        out_ref[0, 1] = (base - zw_b) * rb + zw_b * near_b

    lower = lambda j: (j, 0, 0)
    upper = lambda j: (node_count - 1 - j, 0, 0)
    slab = (1, pair_count, cell_count)
    smem = pl.BlockSpec(memory_space=pltpu.SMEM)
    in_specs = [
        smem,
        smem,
        pl.BlockSpec(slab, lower),
        pl.BlockSpec(slab, upper),
        pl.BlockSpec(slab, lower),
        pl.BlockSpec(slab, upper),
        pl.BlockSpec(packet.shape, lambda j: (0, 0)),
        pl.BlockSpec(slab, lambda j: (0, 0, 0)),
        pl.BlockSpec(flip.shape, lambda j: (0, 0)),
    ]
    return pl.pallas_call(
        kernel,
        grid=(steps,),
        in_specs=in_specs,
        out_specs=pl.BlockSpec((1, 2, pair_count, cell_count), lambda j: (j, 0, 0, 0)),
        out_shape=jax.ShapeDtypeStruct((steps, 2, pair_count, cell_count), jnp.float32),
        compiler_params=pltpu.CompilerParams(dimension_semantics=("arbitrary",)),
    )(scalars, faces, field_in, field_in, recon_parts, recon_parts, packet, columns, flip)


def halo_kernel(partial, got_next, got_prev, recon_parts, packet_next, packet_prev, columns, scalars):
    node_count, half, cell_count = got_next.shape
    pair_count = 2 * half
    steps = node_count // 2
    moment_count = packet_next.shape[0] - 3

    def kernel(sc_ref, part_ref, nxt_ref, prv_ref, rec_ref, pn_ref, pp_ref, col_ref, out_ref):
        rate = sc_ref[31]
        pn = pn_ref[...]
        pp = pp_ref[...]
        rec = rec_ref[0]
        up = jnp.dot(rec, cross_matrix(pn, moment_count), preferred_element_type=jnp.float32)[half:]
        down = jnp.dot(rec, cross_matrix(pp, moment_count), preferred_element_type=jnp.float32)[:half]
        keep_up = rate * pn[moment_count + 1 : moment_count + 2, :]
        keep_down = rate * pp[moment_count : moment_count + 1, :]
        up = (keep_up * nxt_ref[0].astype(jnp.float32) + up).astype(jnp.bfloat16)
        down = (keep_down * prv_ref[0].astype(jnp.float32) + down).astype(jnp.bfloat16)
        shifted = jnp.concatenate([down.astype(jnp.float32), up.astype(jnp.float32)], axis=0)
        out_ref[0] = (part_ref[0, 0] + col_ref[0] * shifted).astype(jnp.bfloat16)

    def pair_of(i):
        return (jnp.where(i < steps, i, node_count - 1 - i), jnp.where(i < steps, 0, 1), 0, 0)

    smem = pl.BlockSpec(memory_space=pltpu.SMEM)
    in_specs = [
        smem,
        pl.BlockSpec((1, 1, pair_count, cell_count), pair_of),
        pl.BlockSpec((1, half, cell_count), lambda i: (i, 0, 0)),
        pl.BlockSpec((1, half, cell_count), lambda i: (i, 0, 0)),
        pl.BlockSpec((1, pair_count, cell_count), lambda i: (i, 0, 0)),
        pl.BlockSpec(packet_next.shape, lambda i: (0, 0)),
        pl.BlockSpec(packet_prev.shape, lambda i: (0, 0)),
        pl.BlockSpec((1, pair_count, cell_count), lambda i: (1, 0, 0)),
    ]
    return pl.pallas_call(
        kernel,
        grid=(node_count,),
        in_specs=in_specs,
        out_specs=pl.BlockSpec((1, pair_count, cell_count), lambda i: (i, 0, 0)),
        out_shape=jax.ShapeDtypeStruct((node_count, pair_count, cell_count), jnp.bfloat16),
        compiler_params=pltpu.CompilerParams(dimension_semantics=("arbitrary",)),
    )(scalars, partial, got_next, got_prev, recon_parts, packet_next, packet_prev, columns)


def solution(mesh):
    in_specs = (
        P("species", None, None, "space"),
        P("species"),
        P("species"),
        P(),
        P("space"),
        P("space"),
        P(None, "space"),
    )
    out_specs = P("species", None, None, "space")

    return jax.shard_map(on_device, mesh=mesh, in_specs=in_specs, out_specs=out_specs, check_vma=False)
```

profile of v0, /device:TPU:1, one launch (start us, length us, event | category | flops | bytes accessed | tf_op | source)
XLA Modules:
  0.0 56.1 jit_solution(812428073376964143)
XLA Ops:
  0.0 0.7 %subtract_convert_fusion.2 = (bf16[128]{0:T(256)(128)(2,1)S(1)}, f32[1,128]{1,0:T(1,128)S(1)}) fusion(s32[128]{0:T(128)} %param.15), kind=kLoop, calls=%fused_computation.32 | loop fusion | flops 384 | bytes 1280 | tf_op jit(solution)/shard_map/convert_element_type | solution.py:87
  0.7 0.7 %subtract_multiply_fusion = f32[128]{0:T(128)S(1)} fusion(s32[128]{0:T(128)} %param.16, s32[128]{0:T(128)} %param.15), kind=kLoop, calls=%fused_computation.31 | loop fusion | flops 640 | bytes 1536 | tf_op jit(solution)/shard_map/mul | solution.py:88
  1.3 0.1 select_convert_fusion
  1.5 0.0 copy-start.1
  1.5 1.8 %broadcast_multiply_fusion = bf16[20,400,128]{2,1,0:T(8,128)(2,1)S(1)} fusion(bf16[400,128]{1,0:T(8,128)(2,1)S(1)} %select_convert_fusion, bf16[1,400,20,128]{3,1,2,0:T(8,128)(2,1)} %param.11), kind=kLoop, calls=%fused_computation.3 | loop fusion | flops 1024000 | bytes 4198400 | tf_op jit(solution)/shard_map/mul | solution.py:91
  3.3 0.0 copy-start
  3.3 0.0 copy-done.1
  3.3 0.5 fusion.13
  3.8 3.2 %collective-permute-start.1 = (f32[13,128]{1,0:T(8,128)S(1)}, f32[13,128]{1,0:T(8,128)S(1)}, u32[]{:S(2)}, u32[]{:S(2)}) collective-permute-start(f32[13,128]{1,0:T(8,128)S(1)} %slice_add_fusion.2), channel_id=1, source_target_pairs={{0,2},{1,3},{2,0},{3,1},{4,6},{5,7},{6,4},{7,5},{8,10},{9,11},{10,... | collective-permute-start | bytes 19976 | tf_op jit(solution)/shard_map/ppermute | solution.py:21
  7.0 1.3 %collective-permute-start = (f32[13,128]{1,0:T(8,128)S(1)}, f32[13,128]{1,0:T(8,128)S(1)}, u32[]{:S(2)}, u32[]{:S(2)}) collective-permute-start(f32[13,128]{1,0:T(8,128)S(1)} %slice_add_fusion.2), channel_id=1, source_target_pairs={{0,1},{1,2},{2,3},{3,0},{4,5},{5,6},{6,7},{7,4},{8,9},{9,10},{10,1... | collective-permute-start | bytes 19976 | tf_op jit(solution)/shard_map/ppermute | solution.py:21
  8.3 2.0 %collective-permute-start.2 = (f32[13,128]{1,0:T(8,128)S(1)}, f32[13,128]{1,0:T(8,128)S(1)}, u32[]{:S(2)}, u32[]{:S(2)}) collective-permute-start(f32[13,128]{1,0:T(8,128)S(1)} %slice_add_fusion.2), channel_id=1, source_target_pairs={{0,3},{1,0},{2,1},{3,2},{4,7},{5,4},{6,5},{7,6},{8,11},{9,8},{10,9... | collective-permute-start | bytes 19976 | tf_op jit(solution)/shard_map/ppermute | solution.py:21
  10.3 0.0 copy-done
  10.3 1.5 %fusion.12 = (bf16[20,200,128]{2,1,0:T(8,128)(2,1)}, bf16[20,200,128]{2,1,0:T(8,128)(2,1)}) fusion(bf16[20,400,128]{2,1,0:T(8,128)(2,1)S(1)} %bitcast.30), kind=kLoop, calls=%fused_computation.35 | loop fusion | bytes 4096000 | tf_op jit(solution)/shard_map/slice | solution.py:83
  11.8 2.6 %collective-permute-start.4 = (bf16[20,200,128]{2,1,0:T(8,128)(2,1)}, bf16[20,200,128]{2,1,0:T(8,128)(2,1)S(1)}, u32[]{:S(2)}, u32[]{:S(2)}) collective-permute-start(bf16[20,200,128]{2,1,0:T(8,128)(2,1)} %get-tuple-element.5), channel_id=1, source_target_pairs={{0,4},{4,8},{8,12},{12,16},{16,20},{20,24},{24,28},{28,0},{1,5},{5... | collective-permute-start | bytes 3072008 | tf_op jit(solution)/shard_map/ppermute | solution.py:21
  14.4 0.0 collective-permute-start.3
  14.4 0.8 %fusion.1.flip_ref = bf16[400,400]{1,0:T(8,128)(2,1)} fusion(), kind=kLoop, calls=%fused_computation.5 | loop fusion | flops 480000 | bytes 320000 | tf_op jit(solution)/shard_map/convert_element_type | solution.py:162
  15.8 0.0 copy-done.11
  15.9 0.1 broadcast_in_dim.60
  15.9 0.1 abs.20
  16.1 0.1 convert_element_type.38
  16.1 0.0 copy-done.4
  16.2 0.1 fusion.2
  16.3 0.0 copy-start.8
  16.3 0.7 %fusion.4 = f32[8000,128]{1,0:T(8,128)S(1)} fusion(bf16[13,128]{1,0:T(8,128)(2,1)S(1)} %copy-done.10, f32[13,8000]{1,0:T(8,128)S(1)} %fusion.2), kind=kOutput, calls=%fused_computation.12 | convolution fusion | flops 26728000 | bytes 4515328 | tf_op jit(solution)/shard_map/dot_general | solution.py:153
  17.1 0.0 copy-start.9
  17.1 0.7 %convolution_add_fusion.1 = f32[8000,128]{1,0:T(8,128)S(1)} fusion(f32[8000,128]{1,0:T(8,128)S(1)} %fusion.4, bf16[13,128]{1,0:T(8,128)(2,1)S(1)} %copy-done.8, f32[13,8000]{1,0:T(8,128)S(1)} %fusion.2), kind=kOutput, calls=%fused_computation.1 | convolution fusion | flops 28064000 | bytes 8611328 | tf_op jit(solution)/shard_map/dot_general | solution.py:153
  17.9 2.1 %fusion = bf16[8000,128]{1,0:T(8,128)(2,1)} fusion(f32[8000,128]{1,0:T(8,128)S(1)} %convolution_add_fusion.1, bf16[13,128]{1,0:T(8,128)(2,1)S(1)} %copy-done.9, f32[13,8000]{1,0:T(8,128)S(1)} %fusion.2), kind=kOutput, calls=%fused_computation.2 | convolution fusion | flops 29400000 | bytes 6563328 | tf_op jit(solution)/shard_map/dot_general | solution.py:153
  19.9 0.8 %fusion.7 = (f32[13]{0:T(128)S(1)}, f32[13]{0:T(128)S(1)}, f32[13]{0:T(128)S(1)}, f32[13]{0:T(128)S(1)}) fusion(f32[4,4,13]{2,1,0:T(4,128)} %param.14, s32[]{:T(128)S(6)} %select_n.48, s32[]{:T(128)S(6)} %select_n.52, s32[]{:T(128)S(6)} %select_n.58, s32[]{:T(128)S(6)} %select_n.55), kind=kLoop, calls=%fused_computation.26 | loop fusion | bytes 432 | tf_op jit(solution)/shard_map/mul | solution.py:102
  21.4 0.1 pad.5.clone
  21.5 0.0 collective-permute-done.1
  21.5 0.0 collective-permute-done
  21.5 0.0 collective-permute-done.2
  21.5 0.1 multiply_add_fusion
  21.6 0.1 maximum_maximum_fusion.pk_ref
  21.6 1.7 %collective-permute-start.6 = (f32[16,128]{1,0:T(8,128)S(1)}, f32[16,128]{1,0:T(8,128)S(1)}, u32[]{:S(2)}, u32[]{:S(2)}) collective-permute-start(f32[16,128]{1,0:T(8,128)S(1)} %maximum_maximum_fusion.pk_ref), channel_id=1, source_target_pairs={{0,4},{4,8},{8,12},{12,16},{16,20},{20,24},{24,28},{28,0},{1,5},{5... | collective-permute-start | bytes 24584 | tf_op jit(solution)/shard_map/ppermute | solution.py:21
  23.4 0.0 collective-permute-start.5
  23.4 0.6 %pad_maximum_fusion.1.sc_ref = f32[32]{0:T(128)} fusion(f32[1]{0:T(128)S(6)} %sub.44, f32[11]{0:T(128)S(1)} %broadcast.72, f32[20]{0:T(128)S(1)} %multiply_abs_fusion), kind=kLoop, calls=%fused_computation.30 | loop fusion | flops 64 | bytes 256 | tf_op jit(solution)/shard_map/concatenate | solution.py:132
  24.0 1.0 %broadcast_in_dim.61.col_ref = f32[2,400,128]{2,1,0:T(8,128)} broadcast(f32[2,400]{1,0:T(2,128)S(1)} %pad_maximum_fusion), dimensions={0,1} | broadcast | bytes 412800 | tf_op jit(solution)/shard_map/broadcast_in_dim | solution.py:129
  24.9 10.2 %shard_map.109.part_ref = f32[10,2,400,128]{3,2,1,0:T(8,128)} custom-call(f32[32]{0:T(128)} %pad_maximum_fusion.1.sc_ref, s32[2]{0:T(128)} %bitcast.36, bf16[20,400,128]{2,1,0:T(8,128)(2,1)} %bitcast.28, bf16[20,400,128]{2,1,0:T(8,128)(2,1)} %bitcast.29, bf16[20,400,128]{2,1,0:T(8,128)(2,1)} %bitcast.31, bf16[20,400,128]{2,1,0:T(8,128)(2,1)} %bitcast.32, ...), custom_call_target="tpu_custom_call" | custom-call | tf_op jit(solution)/shard_map/pallas_call | solution.py:232
  35.1 0.4 collective-permute-done.6.pp_ref
  35.5 3.4 %collective-permute-done.5.pn_ref = f32[16,128]{1,0:T(8,128)S(1)} collective-permute-done((f32[16,128]{1,0:T(8,128)S(1)}, f32[16,128]{1,0:T(8,128)S(1)}, u32[]{:S(2)}, u32[]{:S(2)}) %collective-permute-start.5) | collective-permute-done | bytes 8224 | tf_op jit(solution)/shard_map/ppermute | solution.py:21
  38.9 0.0 collective-permute-done.4.prv_ref
  38.9 0.0 collective-permute-done.3.nxt_ref
  38.9 0.0 copy-done.6
  38.9 0.6 %copy-done.7 = f32[16,128]{1,0:T(8,128)} copy-done((f32[16,128]{1,0:T(8,128)}, f32[16,128]{1,0:T(8,128)S(1)}, u32[]{:S(2)}) %copy-start.7) | copy-done | bytes 8216
  39.5 0.4 copy-done.2
  39.9 1.0 %copy-done.3 = bf16[20,200,128]{2,1,0:T(8,128)(2,1)} copy-done((bf16[20,200,128]{2,1,0:T(8,128)(2,1)}, bf16[20,200,128]{2,1,0:T(8,128)(2,1)S(1)}, u32[]{:S(2)}) %copy-start.3) | copy-done | bytes 1024024
  40.9 15.2 %shard_map.110 = bf16[20,400,128]{2,1,0:T(8,128)(2,1)} custom-call(f32[32]{0:T(128)} %pad_maximum_fusion.1.sc_ref, f32[10,2,400,128]{3,2,1,0:T(8,128)} %shard_map.109.part_ref, bf16[20,200,128]{2,1,0:T(8,128)(2,1)} %copy-done.3, bf16[20,200,128]{2,1,0:T(8,128)(2,1)} %copy-done.2, bf16[20,400,128]{2,1,0:T(8,128)(2,1)} %bitcast.33, f32[16,128]{1,0:T(8,128)} %copy-done.7, ...), custom_call_target="tpu_custom_call" | custom-call | tf_op jit(solution)/shard_map/pallas_call | solution.py:276
  (18 shorter events, 0.1 us)
Async XLA Ops:
  1.5 1.8 %copy-start.1 = (bf16[39,8000]{1,0:T(8,128)(2,1)S(1)}, bf16[39,8000]{1,0:T(8,128)(2,1)}, u32[]{:S(2)}) copy-start(bf16[39,8000]{1,0:T(8,128)(2,1)} %constant.141.clone) | copy-start | bytes 1872004
  3.3 7.0 %copy-start = (bf16[1,400,20,128]{3,1,2,0:T(8,128)(2,1)S(1)}, bf16[1,400,20,128]{3,1,2,0:T(8,128)(2,1)}, u32[]{:S(2)}) copy-start(bf16[1,400,20,128]{3,1,2,0:T(8,128)(2,1)} %param.11) | copy-start | bytes 6144004
  3.8 17.6 %collective-permute-start.1 = (f32[13,128]{1,0:T(8,128)S(1)}, f32[13,128]{1,0:T(8,128)S(1)}, u32[]{:S(2)}, u32[]{:S(2)}) collective-permute-start(f32[13,128]{1,0:T(8,128)S(1)} %slice_add_fusion.2), channel_id=1, source_target_pairs={{0,2},{1,3},{2,0},{3,1},{4,6},{5,7},{6,4},{7,5},{8,10},{9,11},{10,... | collective-permute-start | bytes 19976 | tf_op jit(solution)/shard_map/ppermute | solution.py:21
  7.0 14.4 %collective-permute-start = (f32[13,128]{1,0:T(8,128)S(1)}, f32[13,128]{1,0:T(8,128)S(1)}, u32[]{:S(2)}, u32[]{:S(2)}) collective-permute-start(f32[13,128]{1,0:T(8,128)S(1)} %slice_add_fusion.2), channel_id=1, source_target_pairs={{0,1},{1,2},{2,3},{3,0},{4,5},{5,6},{6,7},{7,4},{8,9},{9,10},{10,1... | collective-permute-start | bytes 19976 | tf_op jit(solution)/shard_map/ppermute | solution.py:21
  8.3 13.1 %collective-permute-start.2 = (f32[13,128]{1,0:T(8,128)S(1)}, f32[13,128]{1,0:T(8,128)S(1)}, u32[]{:S(2)}, u32[]{:S(2)}) collective-permute-start(f32[13,128]{1,0:T(8,128)S(1)} %slice_add_fusion.2), channel_id=1, source_target_pairs={{0,3},{1,0},{2,1},{3,2},{4,7},{5,4},{6,5},{7,6},{8,11},{9,8},{10,9... | collective-permute-start | bytes 19976 | tf_op jit(solution)/shard_map/ppermute | solution.py:21
  10.3 5.5 %copy-start.11 = (f32[20]{0:T(128)S(1)}, f32[20]{0:T(128)}, u32[]{:S(2)}) copy-start(f32[20]{0:T(128)} %constant.142.clone) | copy-start | bytes 244
  11.8 4.4 %copy-start.4 = (f32[8000]{0:T(1024)S(1)}, f32[8000]{0:T(1024)}, u32[]{:S(2)}) copy-start(f32[8000]{0:T(1024)} %constant.143.clone) | copy-start | bytes 96004
  11.8 27.1 %collective-permute-start.4 = (bf16[20,200,128]{2,1,0:T(8,128)(2,1)}, bf16[20,200,128]{2,1,0:T(8,128)(2,1)S(1)}, u32[]{:S(2)}, u32[]{:S(2)}) collective-permute-start(bf16[20,200,128]{2,1,0:T(8,128)(2,1)} %get-tuple-element.5), channel_id=1, source_target_pairs={{0,4},{4,8},{8,12},{12,16},{16,20},{20,24},{24,28},{28,0},{1,5},{5... | collective-permute-start | bytes 3072008 | tf_op jit(solution)/shard_map/ppermute | solution.py:21
  14.4 24.5 %collective-permute-start.3 = (bf16[20,200,128]{2,1,0:T(8,128)(2,1)}, bf16[20,200,128]{2,1,0:T(8,128)(2,1)S(1)}, u32[]{:S(2)}, u32[]{:S(2)}) collective-permute-start(bf16[20,200,128]{2,1,0:T(8,128)(2,1)} %get-tuple-element.6), channel_id=1, source_target_pairs={{0,28},{4,0},{8,4},{12,8},{16,12},{20,16},{24,20},{28,24},{1,29},{... | collective-permute-start | bytes 3072008 | tf_op jit(solution)/shard_map/ppermute | solution.py:21
  15.2 1.1 %copy-start.10 = (bf16[13,128]{1,0:T(8,128)(2,1)S(1)}, bf16[13,128]{1,0:T(8,128)(2,1)}, u32[]{:S(2)}) copy-start(bf16[13,128]{1,0:T(8,128)(2,1)} %constant.149) | copy-start | bytes 9988
  16.3 0.8 %copy-start.8 = (bf16[13,128]{1,0:T(8,128)(2,1)S(1)}, bf16[13,128]{1,0:T(8,128)(2,1)}, u32[]{:S(2)}) copy-start(bf16[13,128]{1,0:T(8,128)(2,1)} %constant.150) | copy-start | bytes 9988
  17.1 0.8 %copy-start.9 = (bf16[13,128]{1,0:T(8,128)(2,1)S(1)}, bf16[13,128]{1,0:T(8,128)(2,1)}, u32[]{:S(2)}) copy-start(bf16[13,128]{1,0:T(8,128)(2,1)} %constant.151) | copy-start | bytes 9988
  21.6 3.3 %copy-start.5 = (f32[16,128]{1,0:T(8,128)}, f32[16,128]{1,0:T(8,128)S(1)}, u32[]{:S(2)}) copy-start(f32[16,128]{1,0:T(8,128)S(1)} %maximum_maximum_fusion.pk_ref) | copy-start | bytes 24580
  21.6 13.9 %collective-permute-start.6 = (f32[16,128]{1,0:T(8,128)S(1)}, f32[16,128]{1,0:T(8,128)S(1)}, u32[]{:S(2)}, u32[]{:S(2)}) collective-permute-start(f32[16,128]{1,0:T(8,128)S(1)} %maximum_maximum_fusion.pk_ref), channel_id=1, source_target_pairs={{0,4},{4,8},{8,12},{12,16},{16,20},{20,24},{24,28},{28,0},{1,5},{5... | collective-permute-start | bytes 24584 | tf_op jit(solution)/shard_map/ppermute | solution.py:21
  23.4 15.5 %collective-permute-start.5 = (f32[16,128]{1,0:T(8,128)S(1)}, f32[16,128]{1,0:T(8,128)S(1)}, u32[]{:S(2)}, u32[]{:S(2)}) collective-permute-start(f32[16,128]{1,0:T(8,128)S(1)} %maximum_maximum_fusion.pk_ref), channel_id=1, source_target_pairs={{0,28},{4,0},{8,4},{12,8},{16,12},{20,16},{24,20},{28,24},{1,29},{... | collective-permute-start | bytes 24584 | tf_op jit(solution)/shard_map/ppermute | solution.py:21
  35.5 3.4 %copy-start.6 = (f32[16,128]{1,0:T(8,128)}, f32[16,128]{1,0:T(8,128)S(1)}, u32[]{:S(2)}) copy-start(f32[16,128]{1,0:T(8,128)S(1)} %collective-permute-done.6.pp_ref) | copy-start | bytes 24580
  38.9 0.6 %copy-start.7 = (f32[16,128]{1,0:T(8,128)}, f32[16,128]{1,0:T(8,128)S(1)}, u32[]{:S(2)}) copy-start(f32[16,128]{1,0:T(8,128)S(1)} %collective-permute-done.5.pn_ref) | copy-start | bytes 24580
  38.9 1.0 %copy-start.2 = (bf16[20,200,128]{2,1,0:T(8,128)(2,1)}, bf16[20,200,128]{2,1,0:T(8,128)(2,1)S(1)}, u32[]{:S(2)}) copy-start(bf16[20,200,128]{2,1,0:T(8,128)(2,1)S(1)} %collective-permute-done.4.prv_ref) | copy-start | bytes 3072004
  39.9 1.0 %copy-start.3 = (bf16[20,200,128]{2,1,0:T(8,128)(2,1)}, bf16[20,200,128]{2,1,0:T(8,128)(2,1)S(1)}, u32[]{:S(2)}) copy-start(bf16[20,200,128]{2,1,0:T(8,128)(2,1)S(1)} %collective-permute-done.3.nxt_ref) | copy-start | bytes 3072004
where the time goes:
time: 57 us; the launch traced here: 56.1 us
  Pallas kernels  25.4 us (45%)
  starting transfers between devices  10.8 us (19%)
  local copies, waits for them, and re-layouts  5.5 us (10%)
  other arithmetic  5.03 us (9%)
  matrix products  4.06 us (7%)
  waiting for transfers between devices  3.78 us (7%)
  between operations  1.51 us (3%)
    pallas_call x1, Pallas kernels, halo_kernel(): pl.pallas_call(kernel, grid=(node_count,), in_specs=in_specs, out_specs=p...  15.2 us
    ppermute x7, starting transfers between devices, passed_along(): return lax.ppermute(value, axis, pairs)  10.8 us
    pallas_call x1, Pallas kernels, own_kernel(): pl.pallas_call(kernel, grid=(steps,), in_specs=in_specs, out_specs=pl.Blo...  10.2 us
    ppermute x7, waiting for transfers between devices, passed_along(): return lax.ppermute(value, axis, pairs)  3.78 us
    dot_general x3, matrix products, on_device(): lax.dot_general(stacked_parts, jnp.asarray(place, jnp.bfloat16), (((0,),...  3.55 us
    unnamed x24, local copies, waits for them, and re-layouts  2.01 us
    mul x1, other arithmetic, on_device(): masked = field_in * keep.astype(jnp.bfloat16)  1.81 us
    slice x1, local copies, waits for them, and re-layouts, on_device(): lower_in = field_in[:, :half, :]  1.46 us
  transfers between devices with their start and end apart: 7, of which 2 were waited for; matrix products, arithmetic and copies ran while one was open for 16% of the time, Pallas kernels for 18%

commit v1 on v0

--- a/solution.py
+++ b/solution.py
@@ -161,8 +161,14 @@
     flip_cols = lax.broadcasted_iota(jnp.int32, (pair_count, pair_count), 1)
     flip = (flip_rows + flip_cols == pair_count - 1).astype(jnp.bfloat16)
 
-    partial = own_kernel(field_in, recon_parts, packet, columns, flip, scalars, faces)
-    out = halo_kernel(partial, got_next, got_prev, recon_parts, packet_next, packet_prev, columns, scalars)
+    recon_halves = recon_parts.reshape(node_count, 2, half, lanes)
+    partial_lower, partial_upper = own_kernel(
+        field_in, recon_parts, packet, columns, flip, scalars, faces
+    )
+    out = halo_kernel(
+        partial_lower, partial_upper, got_next, got_prev, recon_halves, packet_next, packet_prev,
+        columns, scalars,
+    )
     return jnp.transpose(out, (1, 0, 2))[None]
 
 
@@ -183,104 +189,140 @@
     half = pair_count // 2
     steps = node_count // 2
     moment_count = packet.shape[0] - 3
-
-    def kernel(sc_ref, face_ref, cot_a, cot_b, rec_a, rec_b, pk_ref, col_ref, flip_ref, out_ref):
-        j = pl.program_id(0)
+    group = 5 if steps % 5 == 0 else 1
+    blocks = steps // group
+
+    def kernel(sc_ref, face_ref, cot_lo, cot_hi, rec_lo, rec_hi, pk_ref, col_ref, flip_ref, out_lo, out_hi):
+        b = pl.program_id(0)
         row = lax.broadcasted_iota(jnp.int32, (pair_count, cell_count), 0)
         lane = lax.broadcasted_iota(jnp.int32, (pair_count, cell_count), 1)
         pk = pk_ref[...]
         rate = sc_ref[31]
         keep = rate * jnp.where(row >= half, pk[moment_count + 1 : moment_count + 2, :], pk[moment_count : moment_count + 1, :])
         own = cross_matrix(pk, moment_count)
+        base = col_ref[0]
+        face_a = face_ref[0] == 1
+        face_b = face_ref[1] == 1
 
         def relax(values, rec):
             rebuilt = jnp.dot(rec, own, preferred_element_type=jnp.float32)
             return (keep * values.astype(jnp.float32) + rebuilt).astype(jnp.bfloat16)
 
-        relaxed_a = relax(cot_a[0], rec_a[0])
-        relaxed_b = relax(cot_b[0], rec_b[0])
-        edges = jnp.where(lane == 0, relaxed_b, relaxed_a)
-        flipped = jnp.dot(flip_ref[...], edges, preferred_element_type=jnp.float32)
-        edges32 = edges.astype(jnp.float32)
-        source_a = jnp.where(face_ref[0] == 1, flipped, edges32)
-        source_b = jnp.where(face_ref[1] == 1, flipped, edges32)
-        ra = relaxed_a.astype(jnp.float32)
-        rb = relaxed_b.astype(jnp.float32)
-        near_a = jnp.where(lane == 0, source_a, pltpu.roll(ra, 1, 1))
-        near_b = jnp.where(lane == cell_count - 1, source_b, pltpu.roll(rb, cell_count - 1, 1))
-        base = col_ref[0]
-        zw_a = sc_ref[j]
-        zw_b = sc_ref[node_count - 1 - j]
-        out_ref[0, 0] = (base - zw_a) * ra + zw_a * near_a
-        out_ref[0, 1] = (base - zw_b) * rb + zw_b * near_b
-
-    lower = lambda j: (j, 0, 0)
-    upper = lambda j: (node_count - 1 - j, 0, 0)
-    slab = (1, pair_count, cell_count)
+        def one(t, carry):
+            u = group - 1 - t
+            j = b * group + t
+            relaxed_a = relax(cot_lo[t], rec_lo[t])
+            relaxed_b = relax(cot_hi[u], rec_hi[u])
+            edges = jnp.where(lane == 0, relaxed_b, relaxed_a)
+            flipped = jnp.dot(flip_ref[...], edges, preferred_element_type=jnp.float32)
+            edges32 = edges.astype(jnp.float32)
+            source_a = jnp.where(face_a, flipped, edges32)
+            source_b = jnp.where(face_b, flipped, edges32)
+            ra = relaxed_a.astype(jnp.float32)
+            rb = relaxed_b.astype(jnp.float32)
+            near_a = jnp.where(lane == 0, source_a, pltpu.roll(ra, 1, 1))
+            near_b = jnp.where(lane == cell_count - 1, source_b, pltpu.roll(rb, cell_count - 1, 1))
+            zw_a = sc_ref[j]
+            zw_b = sc_ref[node_count - 1 - j]
+            out_lo[t] = (base - zw_a) * ra + zw_a * near_a
+            out_hi[u] = (base - zw_b) * rb + zw_b * near_b
+            return carry
+
+        lax.fori_loop(0, group, one, 0)
+
+    block = (group, pair_count, cell_count)
     smem = pl.BlockSpec(memory_space=pltpu.SMEM)
     in_specs = [
         smem,
         smem,
-        pl.BlockSpec(slab, lower),
-        pl.BlockSpec(slab, upper),
-        pl.BlockSpec(slab, lower),
-        pl.BlockSpec(slab, upper),
-        pl.BlockSpec(packet.shape, lambda j: (0, 0)),
-        pl.BlockSpec(slab, lambda j: (0, 0, 0)),
-        pl.BlockSpec(flip.shape, lambda j: (0, 0)),
+        pl.BlockSpec(block, lambda b: (b, 0, 0)),
+        pl.BlockSpec(block, lambda b: (2 * blocks - 1 - b, 0, 0)),
+        pl.BlockSpec(block, lambda b: (b, 0, 0)),
+        pl.BlockSpec(block, lambda b: (2 * blocks - 1 - b, 0, 0)),
+        pl.BlockSpec(packet.shape, lambda b: (0, 0)),
+        pl.BlockSpec((1, pair_count, cell_count), lambda b: (0, 0, 0)),
+        pl.BlockSpec(flip.shape, lambda b: (0, 0)),
     ]
+    out_specs = [
+        pl.BlockSpec(block, lambda b: (b, 0, 0)),
+        pl.BlockSpec(block, lambda b: (blocks - 1 - b, 0, 0)),
+    ]
+    shape = jax.ShapeDtypeStruct((steps, pair_count, cell_count), jnp.float32)
     return pl.pallas_call(
         kernel,
-        grid=(steps,),
+        grid=(blocks,),
         in_specs=in_specs,
-        out_specs=pl.BlockSpec((1, 2, pair_count, cell_count), lambda j: (j, 0, 0, 0)),
-        out_shape=jax.ShapeDtypeStruct((steps, 2, pair_count, cell_count), jnp.float32),
-        compiler_params=pltpu.CompilerParams(dimension_semantics=("arbitrary",)),
+        out_specs=out_specs,
+        out_shape=[shape, shape],
+        compiler_params=pltpu.CompilerParams(
+            dimension_semantics=("arbitrary",), vmem_limit_bytes=48 * 1024 * 1024
+        ),
     )(scalars, faces, field_in, field_in, recon_parts, recon_parts, packet, columns, flip)
 
 
-def halo_kernel(partial, got_next, got_prev, recon_parts, packet_next, packet_prev, columns, scalars):
+def halo_kernel(partial_lower, partial_upper, got_next, got_prev, recon_halves, packet_next, packet_prev, columns, scalars):
     node_count, half, cell_count = got_next.shape
     pair_count = 2 * half
     steps = node_count // 2
     moment_count = packet_next.shape[0] - 3
-
-    def kernel(sc_ref, part_ref, nxt_ref, prv_ref, rec_ref, pn_ref, pp_ref, col_ref, out_ref):
+    group = 5 if steps % 5 == 0 else 1
+    blocks = node_count // group
+    lower_blocks = steps // group
+
+    def kernel(sc_ref, plo_ref, phi_ref, nxt_ref, prv_ref, rec_ref, pn_ref, pp_ref, col_ref, out_ref):
+        i = pl.program_id(0)
         rate = sc_ref[31]
         pn = pn_ref[...]
         pp = pp_ref[...]
-        rec = rec_ref[0]
-        up = jnp.dot(rec, cross_matrix(pn, moment_count), preferred_element_type=jnp.float32)[half:]
-        down = jnp.dot(rec, cross_matrix(pp, moment_count), preferred_element_type=jnp.float32)[:half]
+        next_mat = cross_matrix(pn, moment_count)
+        prev_mat = cross_matrix(pp, moment_count)
         keep_up = rate * pn[moment_count + 1 : moment_count + 2, :]
         keep_down = rate * pp[moment_count : moment_count + 1, :]
-        up = (keep_up * nxt_ref[0].astype(jnp.float32) + up).astype(jnp.bfloat16)
-        down = (keep_down * prv_ref[0].astype(jnp.float32) + down).astype(jnp.bfloat16)
-        shifted = jnp.concatenate([down.astype(jnp.float32), up.astype(jnp.float32)], axis=0)
-        out_ref[0] = (part_ref[0, 0] + col_ref[0] * shifted).astype(jnp.bfloat16)
-
-    def pair_of(i):
-        return (jnp.where(i < steps, i, node_count - 1 - i), jnp.where(i < steps, 0, 1), 0, 0)
-
+        side = col_ref[0]
+
+        def run(part_ref):
+            def one(t, carry):
+                up = jnp.dot(rec_ref[t, 1], next_mat, preferred_element_type=jnp.float32)
+                down = jnp.dot(rec_ref[t, 0], prev_mat, preferred_element_type=jnp.float32)
+                up = (keep_up * nxt_ref[t].astype(jnp.float32) + up).astype(jnp.bfloat16)
+                down = (keep_down * prv_ref[t].astype(jnp.float32) + down).astype(jnp.bfloat16)
+                shifted = jnp.concatenate([down.astype(jnp.float32), up.astype(jnp.float32)], axis=0)
+                out_ref[t] = (part_ref[t] + side * shifted).astype(jnp.bfloat16)
+                return carry
+
+            lax.fori_loop(0, group, one, 0)
+
+        @pl.when(i < lower_blocks)
+        def _():
+            run(plo_ref)
+
+        @pl.when(i >= lower_blocks)
+        def _():
+            run(phi_ref)
+
+    block = (group, pair_count, cell_count)
     smem = pl.BlockSpec(memory_space=pltpu.SMEM)
     in_specs = [
         smem,
-        pl.BlockSpec((1, 1, pair_count, cell_count), pair_of),
-        pl.BlockSpec((1, half, cell_count), lambda i: (i, 0, 0)),
-        pl.BlockSpec((1, half, cell_count), lambda i: (i, 0, 0)),
-        pl.BlockSpec((1, pair_count, cell_count), lambda i: (i, 0, 0)),
+        pl.BlockSpec(block, lambda i: (jnp.minimum(i, lower_blocks - 1), 0, 0)),
+        pl.BlockSpec(block, lambda i: (jnp.maximum(i - lower_blocks, 0), 0, 0)),
+        pl.BlockSpec((group, half, cell_count), lambda i: (i, 0, 0)),
+        pl.BlockSpec((group, half, cell_count), lambda i: (i, 0, 0)),
+        pl.BlockSpec((group, 2, half, recon_halves.shape[3]), lambda i: (i, 0, 0, 0)),
         pl.BlockSpec(packet_next.shape, lambda i: (0, 0)),
         pl.BlockSpec(packet_prev.shape, lambda i: (0, 0)),
         pl.BlockSpec((1, pair_count, cell_count), lambda i: (1, 0, 0)),
     ]
     return pl.pallas_call(
         kernel,
-        grid=(node_count,),
+        grid=(blocks,),
         in_specs=in_specs,
-        out_specs=pl.BlockSpec((1, pair_count, cell_count), lambda i: (i, 0, 0)),
+        out_specs=pl.BlockSpec(block, lambda i: (i, 0, 0)),
         out_shape=jax.ShapeDtypeStruct((node_count, pair_count, cell_count), jnp.bfloat16),
-        compiler_params=pltpu.CompilerParams(dimension_semantics=("arbitrary",)),
-    )(scalars, partial, got_next, got_prev, recon_parts, packet_next, packet_prev, columns)
+        compiler_params=pltpu.CompilerParams(
+            dimension_semantics=("arbitrary",), vmem_limit_bytes=48 * 1024 * 1024
+        ),
+    )(scalars, partial_lower, partial_upper, got_next, got_prev, recon_halves, packet_next, packet_prev, columns)
 
 
 def solution(mesh):

time: 57 us -> 46.1 us (0.81)
  Pallas kernels: 25.4 us -> 13.4 us
  waiting for transfers between devices: 3.78 us -> 8.08 us
  local copies, waits for them, and re-layouts: 5.5 us -> 4.01 us
  other arithmetic: 5.03 us -> 3.78 us
    pallas_call x2, Pallas kernels: 25.4 us -> 13.4 us  [the longest x1 6.89 us: halo_kernel(): pl.pallas_call(kernel, grid=(blocks,), in_specs=in_specs, out_specs=pl.Bl...]
    ppermute x7, waiting for transfers between devices: 3.78 us -> 8.08 us  [passed_along(): return lax.ppermute(value, axis, pairs)]
    broadcast_in_dim x1, local copies, waits for them, and re-layouts: 0.96 us -> 0.16 us  [on_device(): jnp.broadcast_to(jnp.stack([1.0 - adv_x, adv_x])[:, :, None], (2, pair_co...]
    convert_element_type x1, other arithmetic: 0.78 us -> 0.04 us  [on_device(): flip = (flip_rows + flip_cols == pair_count - 1).astype(jnp.bfloat16)]
    unnamed x24 -> x18, local copies, waits for them, and re-layouts: 2.01 us -> 1.33 us
  transfers between devices with their start and end apart: 7 -> 7, of which waited for: 2 -> 2; matrix products, arithmetic and copies ran while one was open for 16% -> 15% of each run, Pallas kernels for 18% -> 14%
where the time goes in v1:
time: 46.1 us; the launch traced here: 45.7 us
  Pallas kernels  13.4 us (29%)
  starting transfers between devices  10.8 us (23%)
  waiting for transfers between devices  8.08 us (18%)
  matrix products  4.07 us (9%)
  local copies, waits for them, and re-layouts  4.01 us (9%)
  other arithmetic  3.78 us (8%)
  between operations  1.55 us (3%)
    ppermute x7, starting transfers between devices, passed_along(): return lax.ppermute(value, axis, pairs)  10.8 us
    ppermute x7, waiting for transfers between devices, passed_along(): return lax.ppermute(value, axis, pairs)  8.08 us
    pallas_call x1, Pallas kernels, halo_kernel(): pl.pallas_call(kernel, grid=(blocks,), in_specs=in_specs, out_specs=pl.Bl...  6.89 us
    pallas_call x1, Pallas kernels, own_kernel(): pl.pallas_call(kernel, grid=(blocks,), in_specs=in_specs, out_specs=out_s...  6.55 us
    dot_general x3, matrix products, on_device(): lax.dot_general(stacked_parts, jnp.asarray(place, jnp.bfloat16), (((0,),...  3.56 us
    mul x1, other arithmetic, on_device(): masked = field_in * keep.astype(jnp.bfloat16)  1.81 us
    slice x1, local copies, waits for them, and re-layouts, on_device(): lower_in = field_in[:, :half, :]  1.44 us
    unnamed x18, local copies, waits for them, and re-layouts  1.33 us
  transfers between devices with their start and end apart: 7, of which 2 were waited for; matrix products, arithmetic and copies ran while one was open for 15% of the time, Pallas kernels for 14%

profile of v1, /device:TPU:1, one launch (start us, length us, event | category | flops | bytes accessed | tf_op | source)
XLA Modules:
  0.0 45.7 jit_solution(3389754160007802396)
XLA Ops:
  0.0 0.7 %subtract_convert_fusion.2 = (bf16[128]{0:T(256)(128)(2,1)S(1)}, f32[1,128]{1,0:T(1,128)S(1)}) fusion(s32[128]{0:T(128)} %param.15), kind=kLoop, calls=%fused_computation.32 | loop fusion | flops 384 | bytes 1280 | tf_op jit(solution)/shard_map/convert_element_type | solution.py:87
  0.7 0.7 %subtract_multiply_fusion = f32[128]{0:T(128)S(1)} fusion(s32[128]{0:T(128)} %param.16, s32[128]{0:T(128)} %param.15), kind=kLoop, calls=%fused_computation.31 | loop fusion | flops 640 | bytes 1536 | tf_op jit(solution)/shard_map/mul | solution.py:88
  1.3 0.1 select_convert_fusion
  1.5 0.0 copy-start.3
  1.5 1.8 %broadcast_multiply_fusion = bf16[20,400,128]{2,1,0:T(8,128)(2,1)S(1)} fusion(bf16[400,128]{1,0:T(8,128)(2,1)S(1)} %select_convert_fusion, bf16[1,400,20,128]{3,1,2,0:T(8,128)(2,1)} %param.11), kind=kLoop, calls=%fused_computation.3 | loop fusion | flops 1024000 | bytes 4198400 | tf_op jit(solution)/shard_map/mul | solution.py:91
  3.3 0.0 copy-start.2
  3.3 0.0 copy-done.3
  3.3 0.5 %fusion.13 = f32[39,128]{1,0:T(8,128)S(1)} fusion(bf16[39,8000]{1,0:T(8,128)(2,1)S(1)} %copy-done.3, bf16[8000,128]{1,0:T(8,128)(2,1)S(1)} %bitcast.36), kind=kOutput, calls=%fused_computation.36 | convolution fusion | flops 79872000 | bytes 2691968 | tf_op jit(solution)/shard_map/dot_general | solution.py:92
  3.8 3.2 %collective-permute-start.1 = (f32[13,128]{1,0:T(8,128)S(1)}, f32[13,128]{1,0:T(8,128)S(1)}, u32[]{:S(2)}, u32[]{:S(2)}) collective-permute-start(f32[13,128]{1,0:T(8,128)S(1)} %slice_add_fusion.2), channel_id=1, source_target_pairs={{0,2},{1,3},{2,0},{3,1},{4,6},{5,7},{6,4},{7,5},{8,10},{9,11},{10,... | collective-permute-start | bytes 19976 | tf_op jit(solution)/shard_map/ppermute | solution.py:21
  7.0 1.3 %collective-permute-start = (f32[13,128]{1,0:T(8,128)S(1)}, f32[13,128]{1,0:T(8,128)S(1)}, u32[]{:S(2)}, u32[]{:S(2)}) collective-permute-start(f32[13,128]{1,0:T(8,128)S(1)} %slice_add_fusion.2), channel_id=1, source_target_pairs={{0,1},{1,2},{2,3},{3,0},{4,5},{5,6},{6,7},{7,4},{8,9},{9,10},{10,1... | collective-permute-start | bytes 19976 | tf_op jit(solution)/shard_map/ppermute | solution.py:21
  8.3 2.0 %collective-permute-start.2 = (f32[13,128]{1,0:T(8,128)S(1)}, f32[13,128]{1,0:T(8,128)S(1)}, u32[]{:S(2)}, u32[]{:S(2)}) collective-permute-start(f32[13,128]{1,0:T(8,128)S(1)} %slice_add_fusion.2), channel_id=1, source_target_pairs={{0,3},{1,0},{2,1},{3,2},{4,7},{5,4},{6,5},{7,6},{8,11},{9,8},{10,9... | collective-permute-start | bytes 19976 | tf_op jit(solution)/shard_map/ppermute | solution.py:21
  10.3 0.0 copy-done.2
  10.3 1.4 %fusion.12 = (bf16[20,200,128]{2,1,0:T(8,128)(2,1)}, bf16[20,200,128]{2,1,0:T(8,128)(2,1)}) fusion(bf16[20,400,128]{2,1,0:T(8,128)(2,1)S(1)} %bitcast.32), kind=kLoop, calls=%fused_computation.35 | loop fusion | bytes 4096000 | tf_op jit(solution)/shard_map/slice | solution.py:83
  11.7 2.6 %collective-permute-start.4 = (bf16[20,200,128]{2,1,0:T(8,128)(2,1)}, bf16[20,200,128]{2,1,0:T(8,128)(2,1)S(1)}, u32[]{:S(2)}, u32[]{:S(2)}) collective-permute-start(bf16[20,200,128]{2,1,0:T(8,128)(2,1)} %get-tuple-element.9), channel_id=1, source_target_pairs={{0,4},{4,8},{8,12},{12,16},{16,20},{20,24},{24,28},{28,0},{1,5},{5... | collective-permute-start | bytes 3072008 | tf_op jit(solution)/shard_map/ppermute | solution.py:21
  14.4 0.0 collective-permute-start.3
  14.4 0.0 copy-start.7
  15.1 0.0 copy-done.8
  15.1 0.1 broadcast_in_dim.60
  15.2 0.1 abs.20
  15.3 0.1 convert_element_type.38
  15.4 0.0 copy-done.4
  15.4 0.1 fusion.2
  15.6 0.0 copy-done.7
  15.6 0.0 copy-start.5
  15.6 0.7 %fusion.4 = f32[8000,128]{1,0:T(8,128)S(1)} fusion(bf16[13,128]{1,0:T(8,128)(2,1)S(1)} %copy-done.7, f32[13,8000]{1,0:T(8,128)S(1)} %fusion.2), kind=kOutput, calls=%fused_computation.12 | convolution fusion | flops 26728000 | bytes 4515328 | tf_op jit(solution)/shard_map/dot_general | solution.py:153
  16.3 0.0 copy-done.5
  16.3 0.0 copy-start.6
  16.3 0.7 %convolution_add_fusion.1 = f32[8000,128]{1,0:T(8,128)S(1)} fusion(f32[8000,128]{1,0:T(8,128)S(1)} %fusion.4, bf16[13,128]{1,0:T(8,128)(2,1)S(1)} %copy-done.5, f32[13,8000]{1,0:T(8,128)S(1)} %fusion.2), kind=kOutput, calls=%fused_computation.1 | convolution fusion | flops 28064000 | bytes 8611328 | tf_op jit(solution)/shard_map/dot_general | solution.py:153
  17.1 0.0 copy-start.1
  17.1 2.1 %fusion = bf16[8000,128]{1,0:T(8,128)(2,1)} fusion(f32[8000,128]{1,0:T(8,128)S(1)} %convolution_add_fusion.1, bf16[13,128]{1,0:T(8,128)(2,1)S(1)} %copy-done.6, f32[13,8000]{1,0:T(8,128)S(1)} %fusion.2), kind=kOutput, calls=%fused_computation.2 | convolution fusion | flops 29400000 | bytes 6563328 | tf_op jit(solution)/shard_map/dot_general | solution.py:153
  19.2 0.8 %fusion.7 = (f32[13]{0:T(128)S(1)}, f32[13]{0:T(128)S(1)}, f32[13]{0:T(128)S(1)}, f32[13]{0:T(128)S(1)}) fusion(f32[4,4,13]{2,1,0:T(4,128)} %param.14, s32[]{:T(128)S(6)} %select_n.48, s32[]{:T(128)S(6)} %select_n.52, s32[]{:T(128)S(6)} %select_n.58, s32[]{:T(128)S(6)} %select_n.55), kind=kLoop, calls=%fused_computation.26 | loop fusion | bytes 432 | tf_op jit(solution)/shard_map/mul | solution.py:102
  20.7 0.1 pad.5.clone
  20.8 0.0 collective-permute-done.1
  20.8 0.0 collective-permute-done
  20.8 0.0 collective-permute-done.2
  20.8 0.1 multiply_add_fusion
  20.8 0.1 maximum_maximum_fusion.pk_ref
  20.9 1.7 %collective-permute-start.6 = (f32[16,128]{1,0:T(8,128)S(1)}, f32[16,128]{1,0:T(8,128)S(1)}, u32[]{:S(2)}, u32[]{:S(2)}) collective-permute-start(f32[16,128]{1,0:T(8,128)S(1)} %maximum_maximum_fusion.pk_ref), channel_id=1, source_target_pairs={{0,4},{4,8},{8,12},{12,16},{16,20},{20,24},{24,28},{28,0},{1,5},{5... | collective-permute-start | bytes 24584 | tf_op jit(solution)/shard_map/ppermute | solution.py:21
  22.7 0.0 collective-permute-start.5
  22.7 0.1 pad_maximum_fusion.1.sc_ref
  22.8 0.2 broadcast_in_dim.61.col_ref
  22.9 6.6 %shard_map.109 = (f32[10,400,128]{2,1,0:T(8,128)S(1)}, f32[10,400,128]{2,1,0:T(8,128)S(1)}) custom-call(f32[32]{0:T(128)S(1)} %pad_maximum_fusion.1.sc_ref, s32[2]{0:T(128)S(1)} %bitcast.29, bf16[20,400,128]{2,1,0:T(8,128)(2,1)} %bitcast.30, bf16[20,400,128]{2,1,0:T(8,128)(2,1)} %bitcast.31, bf16[20,400,128]{2,1,0:T(8,128)(2,1)} %bitcast.33, ...), custom_call_target="tpu_custom_call" | custom-call | tf_op jit(solution)/shard_map/pallas_call | solution.py:251
  29.5 1.3 %copy-done = f32[10,400,128]{2,1,0:T(8,128)} copy-done((f32[10,400,128]{2,1,0:T(8,128)}, f32[10,400,128]{2,1,0:T(8,128)S(1)}, u32[]{:S(2)}) %copy-start) | copy-done | bytes 2048024
  30.8 4.7 %collective-permute-done.6.pp_ref = f32[16,128]{1,0:T(8,128)S(1)} collective-permute-done((f32[16,128]{1,0:T(8,128)S(1)}, f32[16,128]{1,0:T(8,128)S(1)}, u32[]{:S(2)}, u32[]{:S(2)}) %collective-permute-start.6) | collective-permute-done | bytes 8224 | tf_op jit(solution)/shard_map/ppermute | solution.py:21
  35.5 3.4 %collective-permute-done.5.pn_ref = f32[16,128]{1,0:T(8,128)S(1)} collective-permute-done((f32[16,128]{1,0:T(8,128)S(1)}, f32[16,128]{1,0:T(8,128)S(1)}, u32[]{:S(2)}, u32[]{:S(2)}) %collective-permute-start.5) | collective-permute-done | bytes 8224 | tf_op jit(solution)/shard_map/ppermute | solution.py:21
  38.8 0.0 collective-permute-done.4.prv_ref
  38.9 0.0 collective-permute-done.3.nxt_ref
  38.9 6.9 %shard_map.110 = bf16[20,400,128]{2,1,0:T(8,128)(2,1)} custom-call(f32[32]{0:T(128)S(1)} %pad_maximum_fusion.1.sc_ref, f32[10,400,128]{2,1,0:T(8,128)S(1)} %get-tuple-element.7.plo_ref, f32[10,400,128]{2,1,0:T(8,128)} %copy-done, bf16[20,200,128]{2,1,0:T(8,128)(2,1)S(1)} %collective-permute-done.3.nxt_ref, ...), custom_call_target="tpu_custom_call" | custom-call | tf_op jit(solution)/shard_map/pallas_call | solution.py:316
  (12 shorter events, 0.1 us)
Async XLA Ops:
  1.5 1.8 %copy-start.3 = (bf16[39,8000]{1,0:T(8,128)(2,1)S(1)}, bf16[39,8000]{1,0:T(8,128)(2,1)}, u32[]{:S(2)}) copy-start(bf16[39,8000]{1,0:T(8,128)(2,1)} %constant.141.clone) | copy-start | bytes 1872004
  3.3 7.0 %copy-start.2 = (bf16[1,400,20,128]{3,1,2,0:T(8,128)(2,1)S(1)}, bf16[1,400,20,128]{3,1,2,0:T(8,128)(2,1)}, u32[]{:S(2)}) copy-start(bf16[1,400,20,128]{3,1,2,0:T(8,128)(2,1)} %param.11) | copy-start | bytes 6144004
  3.8 16.9 %collective-permute-start.1 = (f32[13,128]{1,0:T(8,128)S(1)}, f32[13,128]{1,0:T(8,128)S(1)}, u32[]{:S(2)}, u32[]{:S(2)}) collective-permute-start(f32[13,128]{1,0:T(8,128)S(1)} %slice_add_fusion.2), channel_id=1, source_target_pairs={{0,2},{1,3},{2,0},{3,1},{4,6},{5,7},{6,4},{7,5},{8,10},{9,11},{10,... | collective-permute-start | bytes 19976 | tf_op jit(solution)/shard_map/ppermute | solution.py:21
  7.0 13.7 %collective-permute-start = (f32[13,128]{1,0:T(8,128)S(1)}, f32[13,128]{1,0:T(8,128)S(1)}, u32[]{:S(2)}, u32[]{:S(2)}) collective-permute-start(f32[13,128]{1,0:T(8,128)S(1)} %slice_add_fusion.2), channel_id=1, source_target_pairs={{0,1},{1,2},{2,3},{3,0},{4,5},{5,6},{6,7},{7,4},{8,9},{9,10},{10,1... | collective-permute-start | bytes 19976 | tf_op jit(solution)/shard_map/ppermute | solution.py:21
  8.3 12.4 %collective-permute-start.2 = (f32[13,128]{1,0:T(8,128)S(1)}, f32[13,128]{1,0:T(8,128)S(1)}, u32[]{:S(2)}, u32[]{:S(2)}) collective-permute-start(f32[13,128]{1,0:T(8,128)S(1)} %slice_add_fusion.2), channel_id=1, source_target_pairs={{0,3},{1,0},{2,1},{3,2},{4,7},{5,4},{6,5},{7,6},{8,11},{9,8},{10,9... | collective-permute-start | bytes 19976 | tf_op jit(solution)/shard_map/ppermute | solution.py:21
  10.3 4.8 %copy-start.8 = (f32[20]{0:T(128)S(1)}, f32[20]{0:T(128)}, u32[]{:S(2)}) copy-start(f32[20]{0:T(128)} %constant.142.clone) | copy-start | bytes 244
  11.7 3.7 %copy-start.4 = (f32[8000]{0:T(1024)S(1)}, f32[8000]{0:T(1024)}, u32[]{:S(2)}) copy-start(f32[8000]{0:T(1024)} %constant.143.clone) | copy-start | bytes 96004
  11.7 27.1 %collective-permute-start.4 = (bf16[20,200,128]{2,1,0:T(8,128)(2,1)}, bf16[20,200,128]{2,1,0:T(8,128)(2,1)S(1)}, u32[]{:S(2)}, u32[]{:S(2)}) collective-permute-start(bf16[20,200,128]{2,1,0:T(8,128)(2,1)} %get-tuple-element.9), channel_id=1, source_target_pairs={{0,4},{4,8},{8,12},{12,16},{16,20},{20,24},{24,28},{28,0},{1,5},{5... | collective-permute-start | bytes 3072008 | tf_op jit(solution)/shard_map/ppermute | solution.py:21
  14.4 24.5 %collective-permute-start.3 = (bf16[20,200,128]{2,1,0:T(8,128)(2,1)}, bf16[20,200,128]{2,1,0:T(8,128)(2,1)S(1)}, u32[]{:S(2)}, u32[]{:S(2)}) collective-permute-start(bf16[20,200,128]{2,1,0:T(8,128)(2,1)} %get-tuple-element.10), channel_id=1, source_target_pairs={{0,28},{4,0},{8,4},{12,8},{16,12},{20,16},{24,20},{28,24},{1,29},{... | collective-permute-start | bytes 3072008 | tf_op jit(solution)/shard_map/ppermute | solution.py:21
  14.4 1.2 %copy-start.7 = (bf16[13,128]{1,0:T(8,128)(2,1)S(1)}, bf16[13,128]{1,0:T(8,128)(2,1)}, u32[]{:S(2)}) copy-start(bf16[13,128]{1,0:T(8,128)(2,1)} %constant.149) | copy-start | bytes 9988
  15.6 0.8 %copy-start.5 = (bf16[13,128]{1,0:T(8,128)(2,1)S(1)}, bf16[13,128]{1,0:T(8,128)(2,1)}, u32[]{:S(2)}) copy-start(bf16[13,128]{1,0:T(8,128)(2,1)} %constant.150) | copy-start | bytes 9988
  16.3 0.8 %copy-start.6 = (bf16[13,128]{1,0:T(8,128)(2,1)S(1)}, bf16[13,128]{1,0:T(8,128)(2,1)}, u32[]{:S(2)}) copy-start(bf16[13,128]{1,0:T(8,128)(2,1)} %constant.151) | copy-start | bytes 9988
  17.1 5.8 %copy-start.1 = (s32[2,1]{0,1:T(1,128)S(1)}, s32[2,1]{0,1:T(1,128)}, u32[]{:S(2)}) copy-start(s32[2,1]{0,1:T(1,128)} %param.17) | copy-start | bytes 28
  20.9 14.5 %collective-permute-start.6 = (f32[16,128]{1,0:T(8,128)S(1)}, f32[16,128]{1,0:T(8,128)S(1)}, u32[]{:S(2)}, u32[]{:S(2)}) collective-permute-start(f32[16,128]{1,0:T(8,128)S(1)} %maximum_maximum_fusion.pk_ref), channel_id=1, source_target_pairs={{0,4},{4,8},{8,12},{12,16},{16,20},{20,24},{24,28},{28,0},{1,5},{5... | collective-permute-start | bytes 24584 | tf_op jit(solution)/shard_map/ppermute | solution.py:21
  22.7 16.2 %collective-permute-start.5 = (f32[16,128]{1,0:T(8,128)S(1)}, f32[16,128]{1,0:T(8,128)S(1)}, u32[]{:S(2)}, u32[]{:S(2)}) collective-permute-start(f32[16,128]{1,0:T(8,128)S(1)} %maximum_maximum_fusion.pk_ref), channel_id=1, source_target_pairs={{0,28},{4,0},{8,4},{12,8},{16,12},{20,16},{24,20},{28,24},{1,29},{... | collective-permute-start | bytes 24584 | tf_op jit(solution)/shard_map/ppermute | solution.py:21
  29.5 1.3 %copy-start = (f32[10,400,128]{2,1,0:T(8,128)}, f32[10,400,128]{2,1,0:T(8,128)S(1)}, u32[]{:S(2)}) copy-start(f32[10,400,128]{2,1,0:T(8,128)S(1)} %get-tuple-element.8.phi_ref) | copy-start | bytes 6144004

commit v2 on v1

--- a/solution.py
+++ b/solution.py
@@ -98,13 +98,14 @@
 
     species_index = lax.axis_index("species")
     row_k = lax.dynamic_index_in_dim(coupling, species_index, axis=0, keepdims=False)
-    own_weight = lax.dynamic_index_in_dim(row_k, species_index, axis=0, keepdims=False)
-    cross = own_weight[:, None] * moments
-    for shift in range(1, species_count):
-        source = (species_index - shift) % species_count
-        other = passed_along(moments, "species", shift)
-        weight = lax.dynamic_index_in_dim(row_k, source, axis=0, keepdims=False)
-        cross = cross + weight[:, None] * other
+    everyone = lax.all_to_all(
+        jnp.broadcast_to(moments[None], (species_count,) + moments.shape),
+        "species",
+        0,
+        0,
+        tiled=True,
+    )
+    cross = jnp.sum(row_k[:, :, None] * everyone, axis=0)
 
     rows = 16
     assert moment_count + 2 < rows
@@ -134,42 +135,34 @@
     )
     faces = face_type[:, 0]
 
-    basis_run = lax.optimization_barrier(basis_parts).astype(jnp.float32)
-    basis_sum = (
-        basis_run[:moment_count] + basis_run[moment_count : 2 * moment_count]
-    ) + basis_run[2 * moment_count :]
-    recon_all = basis_sum * jnp.asarray(weight_k)[None]
-    r1 = recon_all.astype(jnp.bfloat16)
-    rest = recon_all - r1.astype(jnp.float32)
-    r2 = rest.astype(jnp.bfloat16)
-    r3 = (rest - r2.astype(jnp.float32)).astype(jnp.bfloat16)
     lanes = 128
-    order = [0, 0, 1, 0, 1, 2]
-    place = np.zeros((3 * moment_count, lanes), np.float32)
-    for block, part in enumerate(order):
-        for m in range(moment_count):
-            place[part * moment_count + m, block * rows + m] = 1.0
-    stacked_parts = jnp.concatenate([r1, r2, r3], axis=0)
-    recon_parts = lax.dot_general(
-        stacked_parts,
-        jnp.asarray(place, jnp.bfloat16),
-        (((0,), (0,)), ((), ())),
-        preferred_element_type=jnp.float32,
-    ).astype(jnp.bfloat16).reshape(node_count, pair_count, lanes)
+    recon_halves = jnp.asarray(packed_recon(recon, rows, lanes))
 
     flip_rows = lax.broadcasted_iota(jnp.int32, (pair_count, pair_count), 0)
     flip_cols = lax.broadcasted_iota(jnp.int32, (pair_count, pair_count), 1)
     flip = (flip_rows + flip_cols == pair_count - 1).astype(jnp.bfloat16)
 
-    recon_halves = recon_parts.reshape(node_count, 2, half, lanes)
     partial_lower, partial_upper = own_kernel(
-        field_in, recon_parts, packet, columns, flip, scalars, faces
+        field_in, recon_halves, packet, columns, flip, scalars, faces
     )
     out = halo_kernel(
         partial_lower, partial_upper, got_next, got_prev, recon_halves, packet_next, packet_prev,
         columns, scalars,
     )
     return jnp.transpose(out, (1, 0, 2))[None]
+
+
+def packed_recon(recon, rows, lanes):
+    moment_count, pair_count, node_count = recon.shape
+    half = pair_count // 2
+    table = np.transpose(recon, (2, 1, 0))
+    parts = bf16_split(table, 3)
+    order = [0, 0, 1, 0, 1, 2]
+    packed = np.zeros((node_count, pair_count, lanes), np.float32)
+    for block, part in enumerate(order):
+        packed[:, :, block * rows : block * rows + moment_count] = parts[part]
+    packed = packed.reshape(node_count, 2, half, lanes)
+    return packed.astype(jnp.bfloat16)
 
 
 def cross_matrix(packet, moment_count):
@@ -184,7 +177,7 @@
     return jnp.concatenate([c1, c2, c1, c3, c2, c1, pad], axis=0)
 
 
-def own_kernel(field_in, recon_parts, packet, columns, flip, scalars, faces):
+def own_kernel(field_in, recon_halves, packet, columns, flip, scalars, faces):
     node_count, pair_count, cell_count = field_in.shape
     half = pair_count // 2
     steps = node_count // 2
@@ -204,15 +197,21 @@
         face_a = face_ref[0] == 1
         face_b = face_ref[1] == 1
 
-        def relax(values, rec):
-            rebuilt = jnp.dot(rec, own, preferred_element_type=jnp.float32)
+        def relax(values, rec_ref, at):
+            rebuilt = jnp.concatenate(
+                [
+                    jnp.dot(rec_ref[at, 0], own, preferred_element_type=jnp.float32),
+                    jnp.dot(rec_ref[at, 1], own, preferred_element_type=jnp.float32),
+                ],
+                axis=0,
+            )
             return (keep * values.astype(jnp.float32) + rebuilt).astype(jnp.bfloat16)
 
         def one(t, carry):
             u = group - 1 - t
             j = b * group + t
-            relaxed_a = relax(cot_lo[t], rec_lo[t])
-            relaxed_b = relax(cot_hi[u], rec_hi[u])
+            relaxed_a = relax(cot_lo[t], rec_lo, t)
+            relaxed_b = relax(cot_hi[u], rec_hi, u)
             edges = jnp.where(lane == 0, relaxed_b, relaxed_a)
             flipped = jnp.dot(flip_ref[...], edges, preferred_element_type=jnp.float32)
             edges32 = edges.astype(jnp.float32)
@@ -237,8 +236,8 @@
         smem,
         pl.BlockSpec(block, lambda b: (b, 0, 0)),
         pl.BlockSpec(block, lambda b: (2 * blocks - 1 - b, 0, 0)),
-        pl.BlockSpec(block, lambda b: (b, 0, 0)),
-        pl.BlockSpec(block, lambda b: (2 * blocks - 1 - b, 0, 0)),
+        pl.BlockSpec((group, 2, half, recon_halves.shape[3]), lambda b: (b, 0, 0, 0)),
+        pl.BlockSpec((group, 2, half, recon_halves.shape[3]), lambda b: (2 * blocks - 1 - b, 0, 0, 0)),
         pl.BlockSpec(packet.shape, lambda b: (0, 0)),
         pl.BlockSpec((1, pair_count, cell_count), lambda b: (0, 0, 0)),
         pl.BlockSpec(flip.shape, lambda b: (0, 0)),
@@ -257,7 +256,7 @@
         compiler_params=pltpu.CompilerParams(
             dimension_semantics=("arbitrary",), vmem_limit_bytes=48 * 1024 * 1024
         ),
-    )(scalars, faces, field_in, field_in, recon_parts, recon_parts, packet, columns, flip)
+    )(scalars, faces, field_in, field_in, recon_halves, recon_halves, packet, columns, flip)
 
 
 def halo_kernel(partial_lower, partial_upper, got_next, got_prev, recon_halves, packet_next, packet_prev, columns, scalars):

time: 46.1 us -> 44.8 us (0.972)
  matrix products: 4.07 us -> 0.5 us
  waiting for transfers between devices: 8.08 us -> 11.4 us
  local copies, waits for them, and re-layouts: 4.01 us -> 3.47 us
  starting transfers between devices: 10.8 us -> 10.3 us
    ppermute x7 -> x4, starting transfers between devices: 10.8 us -> 4.92 us  [passed_along(): return lax.ppermute(value, axis, pairs)]
    all_to_all x0 -> x1, starting transfers between devices: none -> 5.41 us  [on_device(): lax.all_to_all(jnp.broadcast_to(moments[None], (species_count,) + moments...]
    dot_general x3 -> x0, matrix products: 3.56 us -> none  [on_device(): lax.dot_general(stacked_parts, jnp.asarray(place, jnp.bfloat16), (((0,),...]
    ppermute x7 -> x4, waiting for transfers between devices: 8.08 us -> 11.4 us  [passed_along(): return lax.ppermute(value, axis, pairs)]
    mul x1, local copies, waits for them, and re-layouts: 0.83 us -> 0.01 us  [on_device(): cross = jnp.sum(row_k[:, :, None] * everyone, axis=0)]
    broadcast_in_dim x0 -> x1, local copies, waits for them, and re-layouts: none -> 0.62 us  [on_device(): jnp.broadcast_to(moments[None], (species_count,) + moments.shape)]
    unnamed x18 -> x12, local copies, waits for them, and re-layouts: 1.33 us -> 1.34 us
  transfers between devices with their start and end apart: 7 -> 5, of which waited for: 2 -> 2; matrix products, arithmetic and copies ran while one was open for 15% -> 4% of each run, Pallas kernels for 14% -> 15%
where the time goes in v2:
time: 44.8 us; the launch traced here: 44.4 us
  Pallas kernels  13.7 us (31%)
  waiting for transfers between devices  11.4 us (25%)
  starting transfers between devices  10.3 us (23%)
  other arithmetic  3.57 us (8%)
  local copies, waits for them, and re-layouts  3.47 us (8%)
  between operations  1.46 us (3%)
  matrix products  0.5 us (1%)
    ppermute x4, waiting for transfers between devices, passed_along(): return lax.ppermute(value, axis, pairs)  11.4 us
    pallas_call x1, Pallas kernels, halo_kernel(): pl.pallas_call(kernel, grid=(blocks,), in_specs=in_specs, out_specs=pl.Bl...  6.89 us
    pallas_call x1, Pallas kernels, own_kernel(): pl.pallas_call(kernel, grid=(blocks,), in_specs=in_specs, out_specs=out_s...  6.77 us
    all_to_all x1, starting transfers between devices, on_device(): lax.all_to_all(jnp.broadcast_to(moments[None], (species_count,) + moments...  5.41 us
    ppermute x4, starting transfers between devices, passed_along(): return lax.ppermute(value, axis, pairs)  4.92 us
    mul x1, other arithmetic, on_device(): masked = field_in * keep.astype(jnp.bfloat16)  1.81 us
    unnamed x12, local copies, waits for them, and re-layouts  1.34 us
    slice x1, local copies, waits for them, and re-layouts, on_device(): lower_in = field_in[:, :half, :]  1.1 us
  transfers between devices with their start and end apart: 5, of which 2 were waited for; matrix products, arithmetic and copies ran while one was open for 4% of the time, Pallas kernels for 15%

profile of v2, /device:TPU:1, one launch (start us, length us, event | category | flops | bytes accessed | tf_op | source)
XLA Modules:
  0.0 44.4 jit_solution(11392357061219875000)
XLA Ops:
  0.0 0.0 copy-start
  0.0 0.7 %subtract_convert_fusion = (bf16[128]{0:T(256)(128)(2,1)S(1)}, f32[1,128]{1,0:T(1,128)S(1)}) fusion(s32[128]{0:T(128)} %param.14), kind=kLoop, calls=%fused_computation.14 | loop fusion | flops 384 | bytes 1280 | tf_op jit(solution)/shard_map/convert_element_type | solution.py:87
  0.7 0.7 %subtract_multiply_fusion = f32[128]{0:T(128)S(1)} fusion(s32[128]{0:T(128)} %param.15, s32[128]{0:T(128)} %param.14), kind=kLoop, calls=%fused_computation.13 | loop fusion | flops 640 | bytes 1536 | tf_op jit(solution)/shard_map/mul | solution.py:88
  1.4 0.1 select_convert_fusion
  1.5 0.0 copy-start.4
  1.5 1.8 %broadcast_multiply_fusion = bf16[20,400,128]{2,1,0:T(8,128)(2,1)S(1)} fusion(bf16[400,128]{1,0:T(8,128)(2,1)S(1)} %select_convert_fusion, bf16[1,400,20,128]{3,1,2,0:T(8,128)(2,1)} %param.10), kind=kLoop, calls=%fused_computation | loop fusion | flops 1024000 | bytes 4198400 | tf_op jit(solution)/shard_map/mul | solution.py:91
  3.3 0.0 copy-start.3
  3.3 0.0 copy-done.4
  3.3 0.5 %fusion.3 = f32[39,128]{1,0:T(8,128)S(1)} fusion(bf16[39,8000]{1,0:T(8,128)(2,1)S(1)} %copy-done.4, bf16[8000,128]{1,0:T(8,128)(2,1)S(1)} %bitcast.22), kind=kOutput, calls=%fused_computation.18 | convolution fusion | flops 79872000 | bytes 2691968 | tf_op jit(solution)/shard_map/dot_general | solution.py:92
  3.8 0.6 %broadcast_in_dim.59 = f32[4,13,128]{2,1,0:T(8,128)} broadcast(f32[13,128]{1,0:T(8,128)S(1)} %slice_add_fusion), dimensions={1,2} | broadcast | bytes 33280 | tf_op jit(solution)/shard_map/broadcast_in_dim | solution.py:102
  4.5 5.4 %all-to-all-start = ((f32[4,13,128]{2,1,0:T(8,128)}), f32[4,13,128]{2,1,0:T(8,128)S(1)}, u32[]{:S(2)}, u32[]{:S(2)}) async-start(f32[4,13,128]{2,1,0:T(8,128)} %broadcast_in_dim.59), calls=%async_computation | async-start | bytes 65536 | tf_op jit(solution)/shard_map/all_to_all | solution.py:101
  9.9 0.0 copy-done.3
  9.9 0.0 copy-start.5
  9.9 0.0 copy-start.2
  9.9 1.1 %fusion.2 = (bf16[20,200,128]{2,1,0:T(8,128)(2,1)}, bf16[20,200,128]{2,1,0:T(8,128)(2,1)S(1)}) fusion(bf16[20,400,128]{2,1,0:T(8,128)(2,1)S(1)} %bitcast.21), kind=kLoop, calls=%fused_computation.17 | loop fusion | bytes 4096000 | tf_op jit(solution)/shard_map/slice | solution.py:83
  11.0 2.1 %collective-permute-start.1 = (bf16[20,200,128]{2,1,0:T(8,128)(2,1)}, bf16[20,200,128]{2,1,0:T(8,128)(2,1)S(1)}, u32[]{:S(2)}, u32[]{:S(2)}) collective-permute-start(bf16[20,200,128]{2,1,0:T(8,128)(2,1)} %get-tuple-element.9), channel_id=1, source_target_pairs={{0,4},{4,8},{8,12},{12,16},{16,20},{20,24},{24,28},{28,0},{1,5},{5... | collective-permute-start | bytes 3072008 | tf_op jit(solution)/shard_map/ppermute | solution.py:21
  13.0 0.0 collective-permute-start
  13.7 0.0 copy-done.5
  13.7 0.1 broadcast_in_dim.63
  13.8 0.1 abs.20
  14.0 0.0 copy-done
  14.6 0.1 pad.5.clone
  14.7 0.0 all-to-all-done
  14.7 0.1 multiply_reduce_fusion
  14.8 0.1 maximum_maximum_fusion.pk_ref
  14.9 2.9 %collective-permute-start.3 = (f32[16,128]{1,0:T(8,128)S(1)}, f32[16,128]{1,0:T(8,128)S(1)}, u32[]{:S(2)}, u32[]{:S(2)}) collective-permute-start(f32[16,128]{1,0:T(8,128)S(1)} %maximum_maximum_fusion.pk_ref), channel_id=1, source_target_pairs={{0,4},{4,8},{8,12},{12,16},{16,20},{20,24},{24,28},{28,0},{1,5},{5... | collective-permute-start | bytes 24584 | tf_op jit(solution)/shard_map/ppermute | solution.py:21
  17.7 0.0 collective-permute-start.2
  17.7 0.1 pad_maximum_fusion.1.sc_ref
  17.8 0.2 broadcast_in_dim.64.col_ref
  18.0 0.0 copy-done.2
  18.0 6.8 %shard_map.100 = (f32[10,400,128]{2,1,0:T(8,128)S(1)}, f32[10,400,128]{2,1,0:T(8,128)S(1)}) custom-call(f32[32]{0:T(128)S(1)} %pad_maximum_fusion.1.sc_ref, s32[2]{0:T(128)S(1)} %bitcast.18, bf16[20,400,128]{2,1,0:T(8,128)(2,1)} %bitcast.19, bf16[20,400,128]{2,1,0:T(8,128)(2,1)} %bitcast.20, bf16[20,2,200,128]{3,2,1,0:T(8,128)(2,1)} %constant.40.clone.rec_lo.rec_hi.rec_ref, ...), custom_call_target="tpu_custom_call" | custom-call | tf_op jit(solution)/shard_map/pallas_call | solution.py:250
  24.8 0.0 copy-start.1
  24.8 1.3 %copy-done.1 = f32[10,400,128]{2,1,0:T(8,128)} copy-done((f32[10,400,128]{2,1,0:T(8,128)}, f32[10,400,128]{2,1,0:T(8,128)S(1)}, u32[]{:S(2)}) %copy-start.1) | copy-done | bytes 2048024
  26.1 8.3 %collective-permute-done.3.pp_ref = f32[16,128]{1,0:T(8,128)S(1)} collective-permute-done((f32[16,128]{1,0:T(8,128)S(1)}, f32[16,128]{1,0:T(8,128)S(1)}, u32[]{:S(2)}, u32[]{:S(2)}) %collective-permute-start.3) | collective-permute-done | bytes 8224 | tf_op jit(solution)/shard_map/ppermute | solution.py:21
  34.4 3.2 %collective-permute-done.2.pn_ref = f32[16,128]{1,0:T(8,128)S(1)} collective-permute-done((f32[16,128]{1,0:T(8,128)S(1)}, f32[16,128]{1,0:T(8,128)S(1)}, u32[]{:S(2)}, u32[]{:S(2)}) %collective-permute-start.2) | collective-permute-done | bytes 8224 | tf_op jit(solution)/shard_map/ppermute | solution.py:21
  37.5 0.0 collective-permute-done.1.prv_ref
  37.5 0.0 collective-permute-done.nxt_ref
  37.5 6.9 %shard_map.101 = bf16[20,400,128]{2,1,0:T(8,128)(2,1)} custom-call(f32[32]{0:T(128)S(1)} %pad_maximum_fusion.1.sc_ref, f32[10,400,128]{2,1,0:T(8,128)S(1)} %get-tuple-element.7.plo_ref, f32[10,400,128]{2,1,0:T(8,128)} %copy-done.1, bf16[20,200,128]{2,1,0:T(8,128)(2,1)S(1)} %collective-permute-done.nxt_ref, ...), custom_call_target="tpu_custom_call" | custom-call | tf_op jit(solution)/shard_map/pallas_call | solution.py:315
  (8 shorter events, 0.1 us)
Async XLA Ops:
  0.0 14.0 %copy-start = (f32[4,4,13]{2,1,0:T(4,128)S(1)}, f32[4,4,13]{2,1,0:T(4,128)}, u32[]{:S(2)}) copy-start(f32[4,4,13]{2,1,0:T(4,128)} %param.13) | copy-start | bytes 2500
  1.5 1.8 %copy-start.4 = (bf16[39,8000]{1,0:T(8,128)(2,1)S(1)}, bf16[39,8000]{1,0:T(8,128)(2,1)}, u32[]{:S(2)}) copy-start(bf16[39,8000]{1,0:T(8,128)(2,1)} %constant.38.clone) | copy-start | bytes 1872004
  3.3 6.6 %copy-start.3 = (bf16[1,400,20,128]{3,1,2,0:T(8,128)(2,1)S(1)}, bf16[1,400,20,128]{3,1,2,0:T(8,128)(2,1)}, u32[]{:S(2)}) copy-start(bf16[1,400,20,128]{3,1,2,0:T(8,128)(2,1)} %param.10) | copy-start | bytes 6144004
  4.5 10.3 %all-to-all-start = ((f32[4,13,128]{2,1,0:T(8,128)}), f32[4,13,128]{2,1,0:T(8,128)S(1)}, u32[]{:S(2)}, u32[]{:S(2)}) async-start(f32[4,13,128]{2,1,0:T(8,128)} %broadcast_in_dim.59), calls=%async_computation | async-start | bytes 65536 | tf_op jit(solution)/shard_map/all_to_all | solution.py:101
  9.9 3.8 %copy-start.5 = (f32[20]{0:T(128)S(1)}, f32[20]{0:T(128)}, u32[]{:S(2)}) copy-start(f32[20]{0:T(128)} %constant.39.clone) | copy-start | bytes 244
  9.9 8.1 %copy-start.2 = (s32[2,1]{0,1:T(1,128)S(1)}, s32[2,1]{0,1:T(1,128)}, u32[]{:S(2)}) copy-start(s32[2,1]{0,1:T(1,128)} %param.16) | copy-start | bytes 28
  11.0 26.5 %collective-permute-start.1 = (bf16[20,200,128]{2,1,0:T(8,128)(2,1)}, bf16[20,200,128]{2,1,0:T(8,128)(2,1)S(1)}, u32[]{:S(2)}, u32[]{:S(2)}) collective-permute-start(bf16[20,200,128]{2,1,0:T(8,128)(2,1)} %get-tuple-element.9), channel_id=1, source_target_pairs={{0,4},{4,8},{8,12},{12,16},{16,20},{20,24},{24,28},{28,0},{1,5},{5... | collective-permute-start | bytes 3072008 | tf_op jit(solution)/shard_map/ppermute | solution.py:21
  13.0 24.5 %collective-permute-start = (bf16[20,200,128]{2,1,0:T(8,128)(2,1)S(1)}, bf16[20,200,128]{2,1,0:T(8,128)(2,1)S(1)}, u32[]{:S(2)}, u32[]{:S(2)}) collective-permute-start(bf16[20,200,128]{2,1,0:T(8,128)(2,1)S(1)} %get-tuple-element.10), channel_id=1, source_target_pairs={{0,28},{4,0},{8,4},{12,8},{16,12},{20,16},{24,20},{28,24},{1,29},{... | collective-permute-start | bytes 3072008 | tf_op jit(solution)/shard_map/ppermute | solution.py:21
  14.9 19.5 %collective-permute-start.3 = (f32[16,128]{1,0:T(8,128)S(1)}, f32[16,128]{1,0:T(8,128)S(1)}, u32[]{:S(2)}, u32[]{:S(2)}) collective-permute-start(f32[16,128]{1,0:T(8,128)S(1)} %maximum_maximum_fusion.pk_ref), channel_id=1, source_target_pairs={{0,4},{4,8},{8,12},{12,16},{16,20},{20,24},{24,28},{28,0},{1,5},{5... | collective-permute-start | bytes 24584 | tf_op jit(solution)/shard_map/ppermute | solution.py:21
  17.7 19.8 %collective-permute-start.2 = (f32[16,128]{1,0:T(8,128)S(1)}, f32[16,128]{1,0:T(8,128)S(1)}, u32[]{:S(2)}, u32[]{:S(2)}) collective-permute-start(f32[16,128]{1,0:T(8,128)S(1)} %maximum_maximum_fusion.pk_ref), channel_id=1, source_target_pairs={{0,28},{4,0},{8,4},{12,8},{16,12},{20,16},{24,20},{28,24},{1,29},{... | collective-permute-start | bytes 24584 | tf_op jit(solution)/shard_map/ppermute | solution.py:21
  24.8 1.3 %copy-start.1 = (f32[10,400,128]{2,1,0:T(8,128)}, f32[10,400,128]{2,1,0:T(8,128)S(1)}, u32[]{:S(2)}) copy-start(f32[10,400,128]{2,1,0:T(8,128)S(1)} %get-tuple-element.8.phi_ref) | copy-start | bytes 6144004
